TPU v7x, 128 devices: a whole 4x4x4 slice. The times are simulated.
128 devices in a mesh: tok: 16 (over x, y), voc: 8 (over z, core).
Axes of the slice: x: 4, y: 4, z: 4, core: 2. Of those that a mesh axis runs over, the one named last changes fastest.
Arguments:
- hidden_rows: bfloat16 [512, 3584], P(('tok', 'voc')), may hold values from -40 to 40
- head_weight: bfloat16 [147456, 3584], P(('tok', 'voc')), may hold values from -0.09375 to 0.09375
- teacher_index: int32 [512, 64], replicated, may hold values from 0 to 147455, as said below
- teacher_logprob: float32 [512, 64], replicated, may hold values from -10 to -4.2
Outputs:
- row_loss: float32 [512], P(('tok', 'voc'))
- head_grad: bfloat16 [147456, 3584], P(('tok', 'voc'))
- input_grad: bfloat16 [512, 3584], P(('tok', 'voc'))
Inputs may be any that keep to these rules, and one draw needn't show every extreme that they name: `teacher_index`: the 64 entries of one token are distinct.
All inputs are finite; a program needn't handle non-finite values.
Results may differ from a plain program's by a relative error of at most 0.015.
Values may be sent and summed in bfloat16 or wider, within the bound.
No kernel may reach another device: no remote copies, remote signals or barrier semaphores. Data moves between devices by JAX's collectives and lax.ppermute only.
A program may use at most 128 MiB of HBM per device.

v0:
```python
import jax
import jax.numpy as jnp
from jax import lax
from jax.sharding import PartitionSpec as P

loss_scale = 256.0


def teacher_target(local, probs, voc_dev):
    blocks = local.shape[0] // 64
    local_b = local.reshape(blocks, 64, local.shape[1])
    probs_b = probs.reshape(blocks, 64, probs.shape[1])
    columns = jnp.arange(voc_dev, dtype=jnp.int32)[None, None, :]

    def one_block(args):
        block_local, block_probs = args
        equal = block_local[:, :, None] == columns
        return jnp.sum(jnp.where(equal, block_probs[:, :, None], 0.0), axis=1)

    return lax.map(one_block, (local_b, probs_b)).reshape(local.shape[0], voc_dev)


def per_device(hidden_rows, head_weight, teacher_index, teacher_logprob):
    voc_dev = head_weight.shape[0]
    tok_dev = hidden_rows.shape[0]
    every = lax.all_gather(hidden_rows, ("tok", "voc"), axis=0, tiled=True)
    logits = lax.dot_general(
        every, head_weight, (((1,), (1,)), ((), ())), preferred_element_type=jnp.float32
    )
    position = lax.axis_index(("tok", "voc"))
    offset = position * voc_dev
    local = teacher_index - offset
    probs = jnp.exp(teacher_logprob)
    target = teacher_target(local, probs, voc_dev)
    part_dot = jnp.sum(logits * target, axis=1)
    local_peak = jnp.max(logits, axis=1)
    peak = lax.pmax(local_peak, ("tok", "voc"))
    summed, dotted = lax.psum(
        (jnp.sum(jnp.exp(logits - peak[:, None]), axis=1), part_dot), ("tok", "voc")
    )
    lse = peak + jnp.log(summed)
    total_p = jnp.sum(probs, axis=1)
    own_term = jnp.sum(probs * teacher_logprob, axis=1)
    loss_all = own_term - dotted + total_p * lse
    row_loss = lax.dynamic_slice_in_dim(loss_all, position * tok_dev, tok_dev, 0)
    grad = (loss_scale * (total_p[:, None] * jnp.exp(logits - lse[:, None]) - target)).astype(
        jnp.bfloat16
    )
    head_grad = lax.dot_general(
        grad, every, (((0,), (0,)), ((), ())), preferred_element_type=jnp.float32
    ).astype(jnp.bfloat16)
    input_sum = lax.psum_scatter(
        jnp.dot(grad, head_weight, preferred_element_type=jnp.float32),
        ("tok", "voc"),
        scatter_dimension=0,
        tiled=True,
    )
    return (row_loss, head_grad, input_sum.astype(jnp.bfloat16))


def solution(mesh):
    placed = (P(("tok", "voc"), None), P(("tok", "voc"), None), P(), P())
    return jax.shard_map(
        per_device,
        mesh=mesh,
        in_specs=placed,
        out_specs=(P(("tok", "voc")), P(("tok", "voc"), None), P(("tok", "voc"), None)),
        check_vma=False,
    )
```

profile of v0, /device:TPU:0, one launch (start us, length us, event | category | flops | bytes accessed | tf_op | source)
XLA Modules:
  0.0 364.6 jit_solution(16396800213007242610)
XLA Ops:
  7.2 0.0 all-gather.3.cloned.1.call-start
  7.2 0.7 all-gather.3.cloned.1.call-update
  7.9 0.9 broadcast_subtract_fusion
  8.8 0.1 copy.11
  9.0 1.0 multiply_reduce_fusion
  9.9 0.1 copy.12
  10.1 28.0 %while.11 = (s32[]{:T(128)}, f32[8,64,1152]{2,1,0:T(8,128)S(1)}, s32[8,64,64]{2,1,0:T(8,128)S(1)}, f32[8,64,64]{2,1,0:T(8,128)S(1)}, s32[]{:T(128)}) while((s32[]{:T(128)}, f32[8,64,1152]{2,1,0:T(8,128)S(1)}, s32[8,64,64]{2,1,0:T(8,128)S(1)}, f32[8,64,64]{2,1,0:T(8,128)S(1)}, s32[]{:T(128)}) %tuple.35), condition=%wide.region_3.4_spmd.clone, body=%wide.region_1.3_spmd.clone.sunk | while | flops 14082050 | bytes 983113 | solution.py:20
  10.1 3.4 select_reduce_fusion.2
  13.6 3.4 select_reduce_fusion.2
  17.1 3.4 select_reduce_fusion.2
  20.6 3.4 select_reduce_fusion.2
  24.1 3.4 select_reduce_fusion.2
  27.6 3.4 select_reduce_fusion.2
  31.1 3.4 select_reduce_fusion.2
  34.6 3.4 select_reduce_fusion.2
  38.1 41.7 %all-gather.3.cloned.1.call-done = bf16[128,4,3584]{2,1,0:T(4,128)(2,1)} async-done(((bf16[1,4,3584]{2,1,0:T(4,128)(2,1)}), bf16[128,4,3584]{2,1,0:T(4,128)(2,1)}) %all-gather.3.cloned.1.call-update) | async-done | bytes 3670032 | tf_op jit(solution)/shard_map/all_gather | solution.py:26
  79.8 6.7 %reshape.26 = bf16[512,3584]{1,0:T(8,128)(2,1)} reshape(bf16[128,4,3584]{2,1,0:T(4,128)(2,1)} %all-gather.3.cloned.1.call-done) | data formatting | bytes 7340032
  86.5 10.9 %fusion.5 = (f32[512]{0:T(512)S(1)}, f32[512,1152]{1,0:T(8,128)}) fusion(bf16[512,3584]{1,0:T(8,128)(2,1)} %reshape.26, bf16[1152,3584]{1,0:T(8,128)(2,1)} %param.7), kind=kOutput, calls=%fused_computation.19 | convolution fusion | flops 4228447744 | bytes 14288896 | tf_op jit(solution)/shard_map/dot_general | solution.py:27
  97.4 62.7 %pmax.7 = f32[512]{0:T(512)S(1)} all-reduce(f32[512]{0:T(512)S(1)} %get-tuple-element.56), channel_id=1, replica_groups=mesh['tok'=16,'voc'=8] {'tok','voc'}, use_global_device_ids=true, to_apply=%region_8.9 | all-reduce | flops 512 | bytes 4096 | tf_op jit(solution)/shard_map/pmax | solution.py:37
  160.1 2.3 fusion.2
  162.4 64.3 %psum.15 = f32[512]{0:T(512)S(1)} all-reduce(f32[512]{0:T(512)S(1)} %get-tuple-element.42), channel_id=1, replica_groups=mesh['tok'=16,'voc'=8] {'tok','voc'}, use_global_device_ids=true, to_apply=%region_10.11 | all-reduce | flops 512 | bytes 4096 | tf_op jit(solution)/shard_map/psum | solution.py:38
  226.7 2.6 fusion.4
  229.3 0.0 copy-start
  229.3 10.4 %fusion.6 = f32[512,3584]{1,0:T(8,128)} fusion(bf16[512,1152]{1,0:T(8,128)(2,1)S(1)} %fusion.4, bf16[1152,3584]{1,0:T(8,128)(2,1)} %param.7), kind=kOutput, calls=%fused_computation.20 | convolution fusion | flops 4227858432 | bytes 16777216 | tf_op jit(solution)/shard_map/dot_general | solution.py:53
  239.7 0.0 copy-done
  239.7 6.7 %convolution_convert_fusion = bf16[1152,3584]{1,0:T(8,128)(2,1)} fusion(bf16[512,1152]{1,0:T(8,128)(2,1)S(1)} %fusion.4, bf16[512,3584]{1,0:T(8,128)(2,1)S(1)} %copy-done), kind=kOutput, calls=%fused_computation.6 | convolution fusion | flops 4231987200 | bytes 13107200 | tf_op jit(solution)/shard_map/dot_general | solution.py:49
  246.4 109.3 %all-reduce.3 = (f32[512]{0:T(512)S(1)}, bf16[512,3584]{1,0:T(8,128)(2,1)}) all-reduce(f32[512]{0:T(512)S(1)} %get-tuple-element.41, f32[512,3584]{1,0:T(8,128)} %fusion.6), channel_id=1, replica_groups=mesh['tok'=16,'voc'=8] {'tok','voc'}, use_global_device_ids=true, to_apply=%region_5.6 | all-reduce | flops 1835520 | bytes 11014144 | tf_op jit(solution)/shard_map/psum | solution.py:38
  355.7 0.6 dynamic_slice.11
  356.3 1.4 dynamic-slice_convert_fusion
  (27 shorter events, 0.4 us)
Async XLA Ops:
  7.2 72.6 %all-gather.3.cloned.1.call-start = ((), (), s32[]{:S(2)}) async-start(), calls=%async_computation | async-start | bytes 3698688 | tf_op jit(solution)/shard_map/all_gather | solution.py:26
  229.3 10.4 %copy-start = (bf16[512,3584]{1,0:T(8,128)(2,1)S(1)}, bf16[512,3584]{1,0:T(8,128)(2,1)}, u32[]{:S(2)}) copy-start(bf16[512,3584]{1,0:T(8,128)(2,1)} %reshape.26) | copy-start | bytes 11010052
Sparse Core Ops, SparseCore 0:
  11.0 68.7 all-gather.2
where the time goes:
time: 365 us
  blocking collectives  236 us (65%)
  waiting for transfers between devices  42.4 us (12%)
  other arithmetic  34 us (9%)
  matrix products  28 us (8%)
  between operations  14.1 us (4%)
  local copies, waits for them, and re-layouts  9.39 us (3%)
    psum x2, blocking collectives, per_device(): lax.psum((jnp.sum(jnp.exp(logits - peak[:, None]), axis=1), part_dot), ('...  174 us
    pmax x1, blocking collectives, per_device(): peak = lax.pmax(local_peak, ('tok', 'voc'))  62.7 us
    all_gather x1, waiting for transfers between devices, per_device(): every = lax.all_gather(hidden_rows, ('tok', 'voc'), axis=0, tiled=True)  41.7 us
    reduce_sum x8, other arithmetic, one_block(): return jnp.sum(jnp.where(equal, block_probs[:, :, None], 0.0), axis=1)  27.2 us
    dot_general x1, matrix products, per_device(): lax.dot_general(every, head_weight, (((1,), (1,)), ((), ())), preferred_e...  10.9 us
    dot_general x1, matrix products, per_device(): jnp.dot(grad, head_weight, preferred_element_type=jnp.float32)  10.4 us
  transfers between devices with their start and end apart: 1, of which 1 were waited for; matrix products, arithmetic and copies ran while one was open for 8% of the time, Pallas kernels for 0%

commit v1 on v0

--- a/solution.py
+++ b/solution.py
@@ -36,7 +36,7 @@
     local_peak = jnp.max(logits, axis=1)
     peak = lax.pmax(local_peak, ("tok", "voc"))
     summed, dotted = lax.psum(
-        (jnp.sum(jnp.exp(logits - peak[:, None]), axis=1), part_dot), ("tok", "voc")
+        lax.psum((jnp.sum(jnp.exp(logits - peak[:, None]), axis=1), part_dot), "voc"), "tok"
     )
     lse = peak + jnp.log(summed)
     total_p = jnp.sum(probs, axis=1)

time: 365 us -> 351 us (0.962)
  blocking collectives: 236 us -> 223 us
    psum x2, blocking collectives: 174 us -> 50.9 us  [the longest x1 36.9 us: per_device(): lax.psum(lax.psum((jnp.sum(jnp.exp(logits - peak[:, None]), axis=1), part...]
    unnamed x0 -> x1, blocking collectives: none -> 109 us
where the time goes in v1:
time: 351 us
  blocking collectives  223 us (64%)
  waiting for transfers between devices  42.4 us (12%)
  other arithmetic  34 us (10%)
  matrix products  28 us (8%)
  between operations  14.1 us (4%)
  local copies, waits for them, and re-layouts  9.38 us (3%)
    unnamed x1, blocking collectives  109 us
    pmax x1, blocking collectives, per_device(): peak = lax.pmax(local_peak, ('tok', 'voc'))  62.7 us
    all_gather x1, waiting for transfers between devices, per_device(): every = lax.all_gather(hidden_rows, ('tok', 'voc'), axis=0, tiled=True)  41.7 us
    psum x1, blocking collectives, per_device(): lax.psum(lax.psum((jnp.sum(jnp.exp(logits - peak[:, None]), axis=1), part...  36.9 us
    reduce_sum x8, other arithmetic, one_block(): return jnp.sum(jnp.where(equal, block_probs[:, :, None], 0.0), axis=1)  27.2 us
    psum x1, blocking collectives, per_device(): lax.psum((jnp.sum(jnp.exp(logits - peak[:, None]), axis=1), part_dot), 'v...  14.1 us
    dot_general x1, matrix products, per_device(): lax.dot_general(every, head_weight, (((1,), (1,)), ((), ())), preferred_e...  10.9 us
    dot_general x1, matrix products, per_device(): jnp.dot(grad, head_weight, preferred_element_type=jnp.float32)  10.4 us
  transfers between devices with their start and end apart: 1, of which 1 were waited for; matrix products, arithmetic and copies ran while one was open for 8% of the time, Pallas kernels for 0%

profile of v1, /device:TPU:0, one launch (start us, length us, event | category | flops | bytes accessed | tf_op | source)
XLA Modules:
  0.0 350.9 jit_solution(10767267447420421417)
XLA Ops:
  7.2 0.0 all-gather.3.cloned.1.call-start
  7.2 0.7 all-gather.3.cloned.1.call-update
  7.9 0.9 broadcast_subtract_fusion
  8.8 0.1 copy.11
  9.0 1.0 multiply_reduce_fusion
  9.9 0.1 copy.12
  10.1 28.0 %while.11 = (s32[]{:T(128)}, f32[8,64,1152]{2,1,0:T(8,128)S(1)}, s32[8,64,64]{2,1,0:T(8,128)S(1)}, f32[8,64,64]{2,1,0:T(8,128)S(1)}, s32[]{:T(128)}) while((s32[]{:T(128)}, f32[8,64,1152]{2,1,0:T(8,128)S(1)}, s32[8,64,64]{2,1,0:T(8,128)S(1)}, f32[8,64,64]{2,1,0:T(8,128)S(1)}, s32[]{:T(128)}) %tuple.36), condition=%wide.region_3.4_spmd.clone, body=%wide.region_1.3_spmd.clone.sunk | while | flops 14082050 | bytes 983113 | solution.py:20
  10.1 3.4 select_reduce_fusion.2
  13.6 3.4 select_reduce_fusion.2
  17.1 3.4 select_reduce_fusion.2
  20.6 3.4 select_reduce_fusion.2
  24.1 3.4 select_reduce_fusion.2
  27.6 3.4 select_reduce_fusion.2
  31.1 3.4 select_reduce_fusion.2
  34.6 3.4 select_reduce_fusion.2
  38.1 41.7 %all-gather.3.cloned.1.call-done = bf16[128,4,3584]{2,1,0:T(4,128)(2,1)} async-done(((bf16[1,4,3584]{2,1,0:T(4,128)(2,1)}), bf16[128,4,3584]{2,1,0:T(4,128)(2,1)}) %all-gather.3.cloned.1.call-update) | async-done | bytes 3670032 | tf_op jit(solution)/shard_map/all_gather | solution.py:26
  79.8 6.7 %reshape.26 = bf16[512,3584]{1,0:T(8,128)(2,1)} reshape(bf16[128,4,3584]{2,1,0:T(4,128)(2,1)} %all-gather.3.cloned.1.call-done) | data formatting | bytes 7340032
  86.5 10.9 %fusion.5 = (f32[512]{0:T(512)S(1)}, f32[512,1152]{1,0:T(8,128)}) fusion(bf16[512,3584]{1,0:T(8,128)(2,1)} %reshape.26, bf16[1152,3584]{1,0:T(8,128)(2,1)} %param.7), kind=kOutput, calls=%fused_computation.19 | convolution fusion | flops 4228447744 | bytes 14288896 | tf_op jit(solution)/shard_map/dot_general | solution.py:27
  97.4 62.7 %pmax.7 = f32[512]{0:T(512)S(1)} all-reduce(f32[512]{0:T(512)S(1)} %get-tuple-element.60), channel_id=1, replica_groups=mesh['tok'=16,'voc'=8] {'tok','voc'}, use_global_device_ids=true, to_apply=%region_9.10 | all-reduce | flops 512 | bytes 4096 | tf_op jit(solution)/shard_map/pmax | solution.py:37
  160.1 2.3 fusion.2
  162.4 14.1 %all-reduce.2 = (f32[512]{0:T(512)S(1)}, f32[512]{0:T(512)S(1)}) all-reduce(f32[512]{0:T(512)S(1)} %get-tuple-element.42, f32[512]{0:T(512)S(1)} %get-tuple-element.41), channel_id=1, replica_groups=mesh['tok'=16,'voc'=8] {'voc'}, use_global_device_ids=true, to_apply=%region_11.12 | all-reduce | flops 1024 | bytes 8192 | tf_op jit(solution)/shard_map/psum | solution.py:39
  176.5 36.9 %all-reduce.1 = (f32[512]{0:T(512)S(1)}, f32[512]{0:T(512)S(1)}) all-reduce(f32[512]{0:T(512)S(1)} %get-tuple-element.55, f32[512]{0:T(512)S(1)} %get-tuple-element.56), channel_id=1, replica_groups=mesh['tok'=16,'voc'=8] {'tok'}, use_global_device_ids=true, to_apply=%region_12.13 | all-reduce | flops 1024 | bytes 8192 | tf_op jit(solution)/shard_map/psum | solution.py:38
  213.4 2.6 fusion.4
  215.9 0.0 copy-start
  216.0 10.4 %fusion.6 = f32[512,3584]{1,0:T(8,128)} fusion(bf16[512,1152]{1,0:T(8,128)(2,1)S(1)} %fusion.4, bf16[1152,3584]{1,0:T(8,128)(2,1)} %param.7), kind=kOutput, calls=%fused_computation.20 | convolution fusion | flops 4227858432 | bytes 16777216 | tf_op jit(solution)/shard_map/dot_general | solution.py:53
  226.4 0.0 copy-done
  226.4 6.7 %convolution_convert_fusion = bf16[1152,3584]{1,0:T(8,128)(2,1)} fusion(bf16[512,1152]{1,0:T(8,128)(2,1)S(1)} %fusion.4, bf16[512,3584]{1,0:T(8,128)(2,1)S(1)} %copy-done), kind=kOutput, calls=%fused_computation.6 | convolution fusion | flops 4231987200 | bytes 13107200 | tf_op jit(solution)/shard_map/dot_general | solution.py:49
  233.1 109.0 %all-reduce.4 = bf16[512,3584]{1,0:T(8,128)(2,1)} all-reduce(f32[512,3584]{1,0:T(8,128)} %fusion.6), channel_id=2, replica_groups=mesh['tok'=16,'voc'=8] {'tok','voc'}, use_global_device_ids=true, to_apply=%region_13.14.clone | all-reduce | flops 1835008 | bytes 11010048
  342.0 1.4 dynamic-slice_convert_fusion
  343.5 0.6 dynamic_slice.11
  (26 shorter events, 0.4 us)
Async XLA Ops:
  7.2 72.6 %all-gather.3.cloned.1.call-start = ((), (), s32[]{:S(2)}) async-start(), calls=%async_computation | async-start | bytes 3698688 | tf_op jit(solution)/shard_map/all_gather | solution.py:26
  215.9 10.4 %copy-start = (bf16[512,3584]{1,0:T(8,128)(2,1)S(1)}, bf16[512,3584]{1,0:T(8,128)(2,1)}, u32[]{:S(2)}) copy-start(bf16[512,3584]{1,0:T(8,128)(2,1)} %reshape.26) | copy-start | bytes 11010052
Sparse Core Ops, SparseCore 0:
  11.0 68.7 all-gather.2
